TPU v7x, 32 devices: a whole 2x2x4 slice. The times are simulated.
32 devices in a mesh: ctx: 8 (over y, x, core), dp: 4 (over z).
Axes of the slice: x: 2, y: 2, z: 4, core: 2. Of those that a mesh axis runs over, the one named last changes fastest.
Arguments:
- tokens: bfloat16 [4, 1024, 4096], P('dp', 'ctx'), may hold values from -64 to 64
- query_weight: bfloat16 [4096, 4096], P('dp', 'ctx'), may hold values from -0.09375 to 0.09375
- keyval_matrix: bfloat16 [4096, 1024], P('dp', 'ctx'), may hold values from -0.09375 to 0.09375
- grad_out: bfloat16 [4, 1024, 4096], P('dp', 'ctx'), may hold values from -6 to 6
- blocks: int32 [4, 8, 8], replicated, may hold values from 0 to 7, as said below
- counts: int32 [4, 8], replicated, may hold values from 4 to 8, as said below
Outputs:
- attended: bfloat16 [4, 1024, 4096], P('dp', 'ctx')
- grad_query_weight: float32 [4096, 4096], P('dp', 'ctx')
- grad_keyval_weight: float32 [4096, 1024], P('dp', 'ctx')
Inputs may be any that keep to these rules, and one draw needn't show every extreme that they name: For key head g and query block i, the first counts[g, i] entries of blocks[g, i] are distinct; they are the blocks i - 1, i, i + 1, 0 and 7 that exist, then random others. Entries from counts[g, i] on are block numbers that are not attended. counts[g, i] is the number of distinct blocks among i - 1, i, i + 1, 0 and 7 that exist, plus 1 to 3.
All inputs are finite; a program needn't handle non-finite values.
Results may differ from a plain program's by a relative error of at most 0.004.
The roundings to bfloat16 on the way count: a program that leaves them out, or rounds other values in their place, can miss the bound.
Values may be sent and summed in bfloat16 or wider, within the bound.
No kernel may reach another device: no remote copies, remote signals or barrier semaphores. Data moves between devices by JAX's collectives and lax.ppermute only.
A program may use at most 128 MiB of HBM per device.

v0:
```python
import jax
import jax.numpy as jnp
from jax import lax
from jax.sharding import PartitionSpec as P


def partner(block, axis, distance):
    count = lax.axis_size(axis)
    route = []
    for low in range(count):
        high = low | 1 << distance
        if high != low and high < count:
            route += [(low, high), (high, low)]
    return lax.ppermute(block, axis, route)


def attend_part(query_rows, key_rows, vals, dout, valid, scale):
    scores = (
        jnp.einsum("nqhd,nkcd->nhqkc", query_rows, key_rows, preferred_element_type=jnp.float32)
        * scale
    )
    scores = jnp.where(valid[:, None, None, :, None], scores, -jnp.inf)
    peak = jnp.max(scores, axis=(3, 4), keepdims=True)
    expo = jnp.exp(scores - peak)
    probs = expo / jnp.sum(expo, axis=(3, 4), keepdims=True)
    probs_b = probs.astype(jnp.bfloat16)
    out = jnp.einsum("nhqkc,nkcd->nqhd", probs_b, vals, preferred_element_type=jnp.float32).astype(
        jnp.bfloat16
    )
    delta = jnp.transpose(
        jnp.sum(dout.astype(jnp.float32) * out.astype(jnp.float32), axis=3), (0, 2, 1)
    )
    dprob = jnp.einsum("nqhd,nkcd->nhqkc", dout, vals, preferred_element_type=jnp.float32)
    dscore = (probs * (dprob - delta[:, :, :, None, None]) * scale).astype(jnp.bfloat16)
    dquery = jnp.einsum(
        "nhqkc,nkcd->nqhd", dscore, key_rows, preferred_element_type=jnp.float32
    ).astype(jnp.bfloat16)
    dkeys = jnp.einsum("nhqkc,nqhd->nkcd", dscore, query_rows, preferred_element_type=jnp.float32)
    dvals = jnp.einsum("nhqkc,nqhd->nkcd", probs_b, dout, preferred_element_type=jnp.float32)
    return (out, dquery, dkeys, dvals)


def attention(q_heads, keyval_rows, dout_heads, blk, cnt):
    length = q_heads.shape[0]
    head_size = keyval_rows.shape[1] // 2
    heads = q_heads.shape[1] // head_size
    nblocks, kslots = blk.shape
    block = length // nblocks
    scale = head_size ** (-0.5)
    step = 4
    groups = nblocks // step
    key_rows = keyval_rows[:, :head_size].reshape(nblocks, block, head_size)
    vals = keyval_rows[:, head_size:].reshape(nblocks, block, head_size)
    valid = lax.broadcasted_iota(jnp.int32, (nblocks, kslots), 1) < cnt[:, None]
    query_rows = q_heads.reshape(groups, step, block, heads, head_size)
    dout = dout_heads.reshape(groups, step, block, heads, head_size)

    def one_step(args):
        q_part, d_part, b_part, v_part = args
        return attend_part(q_part, key_rows[b_part], vals[b_part], d_part, v_part, scale)

    out, dquery, dkeys, dvals = lax.map(
        one_step,
        (query_rows, dout, blk.reshape(groups, step, kslots), valid.reshape(groups, step, kslots)),
    )
    dkeys = dkeys.reshape(nblocks, kslots, block, head_size)
    dvals = dvals.reshape(nblocks, kslots, block, head_size)
    onehot = (
        (blk[None, :, :] == lax.broadcasted_iota(jnp.int32, (nblocks, 1, 1), 0)) & valid[None]
    ).astype(jnp.float32)
    key_grad = jnp.einsum("bnk,nkcd->bcd", onehot, dkeys, precision=lax.Precision.HIGHEST)
    val_grad = jnp.einsum("bnk,nkcd->bcd", onehot, dvals, precision=lax.Precision.HIGHEST)
    keyval_grad = jnp.concatenate(
        [key_grad.reshape(length, head_size), val_grad.reshape(length, head_size)], axis=1
    )
    return (
        out.reshape(length, heads * head_size),
        dquery.reshape(length, heads * head_size),
        keyval_grad,
    )


def shards(tokens, query_weight, keyval_matrix, grad_out, blocks, counts):
    local_rows = tokens[0]
    group_size = lax.axis_size("ctx") // blocks.shape[0]
    group_bits = group_size.bit_length() - 1
    device = lax.axis_index("ctx")
    query_cols = query_weight.shape[1]
    weights_full = lax.all_gather(
        jnp.concatenate([query_weight, keyval_matrix], axis=1), "dp", axis=0, tiled=True
    )
    query_full = weights_full[:, :query_cols]
    keyval_part = weights_full[:, query_cols:]
    all_rows = lax.all_gather(local_rows, "ctx", axis=0, tiled=True)
    keyval_cols = keyval_part
    for bit in range(group_bits):
        other = partner(keyval_cols, "ctx", bit)
        upper = device >> bit & 1 == 1
        keyval_cols = jnp.where(
            upper,
            jnp.concatenate([other, keyval_cols], axis=1),
            jnp.concatenate([keyval_cols, other], axis=1),
        )
    projected = jnp.dot(
        all_rows,
        jnp.concatenate([query_full, keyval_cols], axis=1),
        preferred_element_type=jnp.float32,
    ).astype(jnp.bfloat16)
    q_heads = projected[:, :query_cols]
    keyval_rows = projected[:, query_cols:]
    dout_heads = lax.all_to_all(grad_out[0], "ctx", split_axis=1, concat_axis=0, tiled=True)
    group_index = device // group_size
    blk = lax.dynamic_index_in_dim(blocks, group_index, 0, keepdims=False)
    cnt = lax.dynamic_index_in_dim(counts, group_index, 0, keepdims=False)
    out_heads, dquery, keyval_grad = attention(q_heads, keyval_rows, dout_heads, blk, cnt)
    attended = lax.all_to_all(out_heads, "ctx", split_axis=0, concat_axis=1, tiled=True)
    summed = keyval_grad
    for bit in range(group_bits):
        summed = summed + partner(summed, "ctx", bit)
    width = summed.shape[1] // group_size
    own_grad = lax.dynamic_slice_in_dim(summed, device % group_size * width, width, 1)
    own_grad = own_grad.astype(jnp.bfloat16)
    contract = (((0,), (0,)), ((), ()))
    grad_query = lax.dot_general(all_rows, dquery, contract, preferred_element_type=jnp.float32)
    grad_keyval = lax.dot_general(all_rows, own_grad, contract, preferred_element_type=jnp.float32)
    grads = lax.psum_scatter(
        jnp.concatenate([grad_query, grad_keyval], axis=1), "dp", scatter_dimension=0, tiled=True
    )
    grad_query = grads[:, :query_cols]
    grad_keyval = grads[:, query_cols:]
    return (attended[None], grad_query, grad_keyval)


def solution(mesh):
    in_specs = (
        P("dp", "ctx", None),
        P("dp", "ctx"),
        P("dp", "ctx"),
        P("dp", "ctx", None),
        P(),
        P(),
    )
    out_specs = (P("dp", "ctx", None), P("dp", "ctx"), P("dp", "ctx"))
    return jax.shard_map(shards, mesh=mesh, in_specs=in_specs, out_specs=out_specs, check_vma=False)
```

profile of v0, /device:TPU:0, one launch (start us, length us, event | category | flops | bytes accessed | tf_op | source)
XLA Modules:
  0.0 476.8 jit_solution(18149583840988707000)
XLA Ops:
  7.2 2.6 pad_maximum_fusion.1
  10.6 100.4 %all-gather.4.cloned.1.call-done = bf16[4096,640]{1,0:T(8,128)(2,1)} async-done(((bf16[1024,640]{1,0:T(8,128)(2,1)}), bf16[4096,640]{1,0:T(8,128)(2,1)}) %all-gather.4.cloned.1.call-update) | async-done | bytes 5242896 | tf_op jit(solution)/shard_map/all_gather | solution.py:89
  111.0 1.3 slice.36
  112.3 1.3 copy.111
  113.6 4.2 all-to-all-start
  120.1 4.6 slice.35
  124.7 2.1 maximum_select_fusion
  126.9 46.3 %all-gather.6.cloned.1.call-done = bf16[1,1024,4096]{2,1,0:T(8,128)(2,1)} async-done(((bf16[1,128,4096]{2,1,0:T(8,128)(2,1)}), bf16[1,1024,4096]{2,1,0:T(8,128)(2,1)}) %all-gather.6.cloned.1.call-update) | async-done | bytes 8388624 | tf_op jit(solution)/shard_map/all_gather | solution.py:94
  173.1 10.4 %fusion.56 = bf16[1024,768]{0,1:T(8,128)(2,1)S(1)} fusion(bf16[1,1024,4096]{2,1,0:T(8,128)(2,1)} %all-gather.6.cloned.1.call-done, bf16[4096,256]{1,0:T(8,128)(2,1)S(1)} %maximum_select_fusion, bf16[4096,512]{1,0:T(8,128)(2,1)} %slice.35), kind=kOutput, calls=%fused_computation.58 | convolution fusion | flops 6455820288 | bytes 16252928 | tf_op jit(solution)/shard_map/dot_general | solution.py:104
  184.0 1.5 reshape.109
  185.6 65.5 %while.16 = (s32[]{:T(128)}, bf16[2,4,128,4,128]{2,4,3,1,0:T(8,128)(2,1)}, bf16[2,4,128,4,128]{4,3,2,1,0:T(4,128)(2,1)}, f32[2,4,8,128,128]{4,3,2,1,0:T(8,128)},...) while((s32[]{:T(128)}, ...), condition=%wide.region_4.5_spmd, body=%wide.region_0.4_spmd.sunk | while | flops 3275222016 | bytes 218726320 | solution.py:62
  186.7 1.2 constant_dynamic-slice_fusion.5
  188.3 1.3 bitcast_reduce_fusion.2
  189.6 1.8 fusion.119
  191.4 3.4 copy-done.6
  194.8 3.2 bitcast_dynamic-update-slice_fusion.8
  198.0 1.9 copy-done.7
  200.7 6.5 %bitcast_dynamic-update-slice_fusion.6 = (bf16[2,4,128,4,128]{2,4,3,1,0:T(8,128)(2,1)}, bf16[4,128,4,128]{3,1,2,0:T(8,128)(2,1)S(1)}) fusion(bf16[2,4,128,4,128]{2,4,3,1,0:T(8,128)(2,1)} %get-tuple-element.241, s32[]{:T(128)} %get-tuple-element.240, bf16[4,8,128,128,1]{3,2,4,1,0:T(8,128)(2,1)S(1)} %bitcast.231, f32[4,4,128]{2,1,0:T(4,128)S(1)} %fusion.119, ...), kind=kOutput, calls=%fused_computation.26.clone.1 | convolution fusion | flops 547618816 | bytes 10502688 | tf_op jit(solution)/shard_map/while/body/eval_jaxpr/nhqkc,nkcd->nqhd/dot_general | solution.py:27
  207.2 1.2 multiply_reduce_fusion.2
  208.5 4.3 fusion.120
  212.8 1.3 bitcast_dynamic-update-slice_fusion.7
  214.1 2.0 copy-done.5
  216.1 0.8 fusion.121
  217.5 1.0 copy-done.10
  219.3 1.2 constant_dynamic-slice_fusion.5
  220.9 1.3 bitcast_reduce_fusion.2
  222.2 1.8 fusion.119
  224.0 3.4 copy-done.6
  227.4 3.2 bitcast_dynamic-update-slice_fusion.8
  230.6 1.9 copy-done.7
  233.3 6.5 %bitcast_dynamic-update-slice_fusion.6 = (bf16[2,4,128,4,128]{2,4,3,1,0:T(8,128)(2,1)}, bf16[4,128,4,128]{3,1,2,0:T(8,128)(2,1)S(1)}) fusion(bf16[2,4,128,4,128]{2,4,3,1,0:T(8,128)(2,1)} %get-tuple-element.241, s32[]{:T(128)} %get-tuple-element.240, bf16[4,8,128,128,1]{3,2,4,1,0:T(8,128)(2,1)S(1)} %bitcast.231, f32[4,4,128]{2,1,0:T(4,128)S(1)} %fusion.119, ...), kind=kOutput, calls=%fused_computation.26.clone.1 | convolution fusion | flops 547618816 | bytes 10502688 | tf_op jit(solution)/shard_map/while/body/eval_jaxpr/nhqkc,nkcd->nqhd/dot_general | solution.py:27
  239.9 1.2 multiply_reduce_fusion.2
  241.1 4.3 fusion.120
  245.5 1.3 bitcast_dynamic-update-slice_fusion.7
  246.7 2.0 copy-done.5
  250.1 1.0 copy-done.10
  251.1 7.2 %fusion.61 = f32[8,128,128]{2,0,1:T(8,128)S(1)} fusion(f32[8,8,128,128]{3,2,1,0:T(8,128)} %bitcast.237, s32[8,8]{0,1:T(8,128)S(1)} %copy-done.14, pred[8,8]{0,1:T(8,128)(4,1)S(1)} %copy-done.15), kind=kOutput, calls=%fused_computation.63 | convolution fusion | flops 100664320 | bytes 4718912 | tf_op jit(solution)/shard_map/bnk,nkcd->bcd/dot_general | solution.py:71
  258.4 5.0 %fusion.64 = f32[8,128,128]{2,0,1:T(8,128)S(1)} fusion(f32[8,8,128,128]{3,2,1,0:T(8,128)S(1)} %bitcast.238, s32[8,8]{0,1:T(8,128)S(1)} %copy-done.14, pred[8,8]{0,1:T(8,128)(4,1)S(1)} %copy-done.15), kind=kOutput, calls=%fused_computation.64 | convolution fusion | flops 100664320 | bytes 4718912 | tf_op jit(solution)/shard_map/bnk,nkcd->bcd/dot_general | solution.py:72
  263.9 10.2 %fusion.38 = f32[4096,512]{0,1:T(8,128)} fusion(bf16[1,1024,4096]{2,1,0:T(8,128)(2,1)} %all-gather.6.cloned.1.call-done, bf16[128,8,4,128]{3,2,1,0:T(4,128)(2,1)S(1)} %bitcast.240), kind=kOutput, calls=%fused_computation.47 | convolution fusion | flops 4294967296 | bytes 17825792 | tf_op jit(solution)/shard_map/dot_general | solution.py:124
  274.1 4.9 %fusion.44 = f32[4096,128]{0,1:T(8,128)S(1)} fusion(bf16[1,1024,4096]{2,1,0:T(8,128)(2,1)} %all-gather.6.cloned.1.call-done, s32[]{:T(128)S(6)} %select_n.51, f32[1024,128]{1,0:T(8,128)S(1)} %bitcast.234, f32[1024,128]{1,0:T(8,128)S(1)} %bitcast.236, f32[1024,256]{1,0:T(8,128)} %collective-permute-done.1), kind=kOutput, calls=%fused_computation.51 | convolution fusion | flops 1074135040 | bytes 12058628 | tf_op jit(solution)/shard_map/dot_general | solution.py:125
  279.0 8.6 %pad_maximum_fusion = f32[4096,640]{0,1:T(8,128)} fusion(f32[4096,128]{0,1:T(8,128)S(1)} %fusion.44, f32[4096,512]{0,1:T(8,128)} %fusion.38), kind=kLoop, calls=%fused_computation.40 | loop fusion | flops 2621440 | bytes 20971520 | tf_op jit(solution)/shard_map/concatenate | solution.py:127
  287.7 1.2 copy-done.13
  289.4 17.9 %all_to_all.32 = bf16[8,128,512]{2,1,0:T(8,128)(2,1)S(1)} all-to-all(bf16[8,128,512]{2,1,0:T(8,128)(2,1)S(1)} %copy.112), channel_id=1, replica_groups=mesh['ctx'=8,'dp'=4] {'ctx'}, dimensions={0} | all-to-all | bytes 2097152 | tf_op jit(solution)/shard_map/all_to_all | solution.py:116
  308.0 1.3 copy.81
  309.3 156.5 %reduce-scatter.2.cloned.1.call-done = f32[1024,640]{0,1:T(8,128)} async-done(((f32[4096,640]{0,1:T(8,128)}), f32[1024,640]{0,1:T(8,128)}) %reduce-scatter.2.cloned.1.call-update) | async-done | bytes 2621456 | tf_op jit(solution)/shard_map/reduce_scatter | solution.py:126
  465.8 1.6 slice-done
  467.4 1.8 copy.82
  469.2 1.0 copy.83
  (92 shorter events, 11.2 us)
Async XLA Ops:
  7.2 111.6 %copy-start = (s32[4,8,8]{2,1,0:T(8,128)S(1)}, s32[4,8,8]{2,1,0:T(8,128)}, u32[]{:S(2)}) copy-start(s32[4,8,8]{2,1,0:T(8,128)} %param.12) | copy-start | bytes 3076
  7.2 105.2 %copy-start.12 = (bf16[1,128,4096]{2,1,0:T(8,128)(2,1)S(1)}, bf16[1,128,4096]{2,1,0:T(8,128)(2,1)}, u32[]{:S(2)}) copy-start(bf16[1,128,4096]{2,1,0:T(8,128)(2,1)} %param.11) | copy-start | bytes 3145732
  7.2 103.8 %all-gather.4.cloned.1.call-start = ((), (), s32[]{:S(2)}) async-start(), calls=%async_computation.3 | async-start | bytes 6553600 | tf_op jit(solution)/shard_map/all_gather | solution.py:89
  9.8 163.3 %all-gather.6.cloned.1.call-start = ((), (), s32[]{:S(2)}) async-start(), calls=%async_computation.5 | async-start | bytes 9437184 | tf_op jit(solution)/shard_map/all_gather | solution.py:94
  112.3 12.5 %collective-permute-start = (bf16[4096,128]{1,0:T(8,128)(2,1)S(1)}, bf16[4096,128]{1,0:T(8,128)(2,1)}, u32[]{:S(2)}, u32[]{:S(2)}) collective-permute-start(bf16[4096,128]{1,0:T(8,128)(2,1)S(1)} %slice.36), channel_id=1, source_target_pairs={{0,4},{4,0},{8,12},{12,8},{16,20},{20,16},{24,28},{28,24},{1,5},{5... | collective-permute-start | bytes 3145736 | tf_op jit(solution)/shard_map/ppermute | solution.py:14
  113.6 71.9 %all-to-all-start = ((bf16[128,8,512]{0,2,1:T(8,128)(2,1)}), bf16[128,8,512]{0,2,1:T(8,128)(2,1)}, u32[]{:S(2)}, u32[]{:S(2)}) async-start(bf16[128,8,512]{0,2,1:T(8,128)(2,1)} %bitcast.39), calls=%async_computation | async-start | bytes 2097152 | tf_op jit(solution)/shard_map/all_to_all | solution.py:111
  117.9 347.9 %reduce-scatter.2.cloned.1.call-start = ((), (), s32[]{:S(2)}) async-start(), calls=%async_computation.4 | async-start | bytes 13107200 | tf_op jit(solution)/shard_map/reduce_scatter | solution.py:126
  185.6 65.5 %copy-start.14 = (s32[8,8]{0,1:T(8,128)S(1)}, s32[8,8]{0,1:T(8,128)}, u32[]{:S(2)}) copy-start(s32[8,8]{0,1:T(8,128)} %copy.76) | copy-start | bytes 772
  185.6 65.5 %copy-start.15 = (pred[8,8]{0,1:T(8,128)(4,1)S(1)}, pred[8,8]{0,1:T(8,128)(4,1)}, u32[]{:S(2)}) copy-start(pred[8,8]{0,1:T(8,128)(4,1)} %iota_compare_fusion.1) | copy-start | bytes 196
  189.5 8.4 %copy-start.2 = (f32[4,8,128,128,4]{3,2,4,1,0:T(8,128)}, f32[4,8,128,128,4]{3,2,4,1,0:T(8,128)S(1)}, u32[]{:S(2)}) copy-start(f32[4,8,128,128,4]{3,2,4,1,0:T(8,128)S(1)} %get-tuple-element.224) | copy-start | bytes 25165828 | tf_op jit(solution)/shard_map/while
  189.6 5.2 %copy-start.6 = (f32[2,4,8,128,128]{4,3,2,1,0:T(8,128)S(1)}, f32[2,4,8,128,128]{4,3,2,1,0:T(8,128)}, u32[]{:S(2)}) copy-start(f32[2,4,8,128,128]{4,3,2,1,0:T(8,128)} %get-tuple-element.244) | copy-start | bytes 12582916 | tf_op jit(solution)/shard_map/while
  198.0 2.0 copy-start.7
  200.7 7.8 %copy-start.3 = (f32[4,8,128,128,4]{3,2,4,1,0:T(8,128)S(1)}, f32[4,8,128,128,4]{3,2,4,1,0:T(8,128)}, u32[]{:S(2)}) copy-start(f32[4,8,128,128,4]{3,2,4,1,0:T(8,128)} %copy-done.2) | copy-start | bytes 25165828 | tf_op jit(solution)/shard_map/while
  208.4 4.4 copy-start.4
  212.8 4.4 copy-start.9
  214.1 2.0 copy-start.5
  217.5 1.0 copy-start.10
  222.2 8.4 %copy-start.2 = (f32[4,8,128,128,4]{3,2,4,1,0:T(8,128)}, f32[4,8,128,128,4]{3,2,4,1,0:T(8,128)S(1)}, u32[]{:S(2)}) copy-start(f32[4,8,128,128,4]{3,2,4,1,0:T(8,128)S(1)} %get-tuple-element.224) | copy-start | bytes 25165828 | tf_op jit(solution)/shard_map/while
  222.2 5.2 %copy-start.6 = (f32[2,4,8,128,128]{4,3,2,1,0:T(8,128)S(1)}, f32[2,4,8,128,128]{4,3,2,1,0:T(8,128)}, u32[]{:S(2)}) copy-start(f32[2,4,8,128,128]{4,3,2,1,0:T(8,128)} %get-tuple-element.244) | copy-start | bytes 12582916 | tf_op jit(solution)/shard_map/while
  230.6 2.0 copy-start.7
  233.3 7.8 %copy-start.3 = (f32[4,8,128,128,4]{3,2,4,1,0:T(8,128)S(1)}, f32[4,8,128,128,4]{3,2,4,1,0:T(8,128)}, u32[]{:S(2)}) copy-start(f32[4,8,128,128,4]{3,2,4,1,0:T(8,128)} %copy-done.2) | copy-start | bytes 25165828 | tf_op jit(solution)/shard_map/while
  241.1 4.4 copy-start.4
  245.4 4.4 copy-start.9
  246.7 2.0 copy-start.5
  250.1 1.0 copy-start.10
  251.1 7.4 %copy-start.8 = (f32[2,4,8,128,128]{4,3,2,1,0:T(8,128)S(1)}, f32[2,4,8,128,128]{4,3,2,1,0:T(8,128)}, u32[]{:S(2)}) copy-start(f32[2,4,8,128,128]{4,3,2,1,0:T(8,128)} %get-tuple-element.66) | copy-start | bytes 12582916
  258.3 5.6 %copy-start.11 = (bf16[2,4,128,4,128]{4,3,2,1,0:T(4,128)(2,1)S(1)}, bf16[2,4,128,4,128]{4,3,2,1,0:T(4,128)(2,1)}, u32[]{:S(2)}) copy-start(bf16[2,4,128,4,128]{4,3,2,1,0:T(4,128)(2,1)} %get-tuple-element.64) | copy-start | bytes 3145732
  263.6 10.5 %collective-permute-start.1 = (f32[1024,256]{1,0:T(8,128)S(1)}, f32[1024,256]{1,0:T(8,128)}, u32[]{:S(2)}, u32[]{:S(2)}) collective-permute-start(f32[1024,256]{1,0:T(8,128)S(1)} %pad_maximum_fusion.2), channel_id=1, source_target_pairs={{0,4},{4,0},{8,12},{12,8},{16,20},{20,16},{24,28},{28,24},{1,5},{5... | collective-permute-start | bytes 3145736 | tf_op jit(solution)/shard_map/ppermute | solution.py:14
  287.6 1.2 copy-start.13
  308.0 162.3 %copy-start.1 = (s32[4,8,8]{2,1,0:T(8,128)S(1)}, s32[4,8,8]{2,1,0:T(8,128)}, u32[]{:S(2)}) copy-start(s32[4,8,8]{2,1,0:T(8,128)} %param.12) | copy-start | bytes 3076
  465.8 1.6 slice-start
  465.8 3.4 slice-start.1
Sparse Core Ops, SparseCore 0:
  10.2 100.7 all-gather.3
  112.8 60.2 all-gather.5
  287.8 178.0 reduce-scatter.1
where the time goes:
time: 478 us; the launch traced here: 477 us
  waiting for transfers between devices  304 us (64%)
  matrix products  72.5 us (15%)
  local copies, waits for them, and re-layouts  43 us (9%)
  other arithmetic  20.1 us (4%)
  blocking collectives  17.9 us (4%)
  between operations  14 us (3%)
    reduce_scatter x1, waiting for transfers between devices, shards(): lax.psum_scatter(jnp.concatenate([grad_query, grad_keyval], axis=1), 'dp'...  157 us
    all_gather x1, waiting for transfers between devices, shards(): lax.all_gather(jnp.concatenate([query_weight, keyval_matrix], axis=1), 'd...  100 us
    all_gather x1, waiting for transfers between devices, shards(): all_rows = lax.all_gather(local_rows, 'ctx', axis=0, tiled=True)  46.3 us
    all_to_all x1, blocking collectives, shards(): lax.all_to_all(out_heads, 'ctx', split_axis=0, concat_axis=1, tiled=True)  17.9 us
    while x32, local copies, waits for them, and re-layouts  16.5 us
    dot_general x2, matrix products, attend_part(): jnp.einsum('nhqkc,nkcd->nqhd', probs_b, vals, preferred_element_type=jnp....  13.1 us
    dot_general x1, matrix products, shards(): jnp.dot(all_rows, jnp.concatenate([query_full, keyval_cols], axis=1), pre...  10.4 us
    dot_general x1, matrix products, shards(): lax.dot_general(all_rows, dquery, contract, preferred_element_type=jnp.fl...  10.2 us
  transfers between devices with their start and end apart: 6, of which 3 were waited for; matrix products, arithmetic and copies ran while one was open for 8% of the time, Pallas kernels for 0%

commit v1 on v0

--- a/solution.py
+++ b/solution.py
@@ -91,7 +91,21 @@
     )
     query_full = weights_full[:, :query_cols]
     keyval_part = weights_full[:, query_cols:]
-    all_rows = lax.all_gather(local_rows, "ctx", axis=0, tiled=True)
+    ways, here, step_2 = (lax.axis_size("ctx"), lax.axis_index("ctx"), local_rows.shape[0])
+    shape = [n * ways if d == 0 else n for d, n in enumerate(local_rows.shape)]
+    full = lax.dynamic_update_slice_in_dim(
+        jnp.zeros(shape, local_rows.dtype), local_rows, here * step_2, axis=0
+    )
+    going_up = going_down = local_rows
+    for far in range(1, ways // 2 + 1):
+        going_up = lax.ppermute(going_up, "ctx", [(d, (d + 1) % ways) for d in range(ways)])
+        full = lax.dynamic_update_slice_in_dim(full, going_up, (here - far) % ways * step_2, axis=0)
+        if 2 * far < ways:
+            going_down = lax.ppermute(going_down, "ctx", [(d, (d - 1) % ways) for d in range(ways)])
+            full = lax.dynamic_update_slice_in_dim(
+                full, going_down, (here + far) % ways * step_2, axis=0
+            )
+    all_rows = full
     keyval_cols = keyval_part
     for bit in range(group_bits):
         other = partner(keyval_cols, "ctx", bit)

time: 478 us -> 413 us (0.86)
  waiting for transfers between devices: 304 us -> 225 us
  starting transfers between devices: 4.76 us -> 15.1 us
  local copies, waits for them, and re-layouts: 43 us -> 50.5 us
    all_gather x1, waiting for transfers between devices: 100 us -> 19.4 us  [shards(): lax.all_gather(jnp.concatenate([query_weight, keyval_matrix], axis=1), 'd...]
    ppermute x0 -> x7, waiting for transfers between devices: none -> 51.8 us  [the longest x4 51.8 us: shards(): lax.ppermute(going_up, 'ctx', [(d, (d + 1) % ways) for d in range(ways)])]
    all_gather x1 -> x0, waiting for transfers between devices: 46.3 us -> none  [shards(): all_rows = lax.all_gather(local_rows, 'ctx', axis=0, tiled=True)]
    dynamic_update_slice x0 -> x8, local copies, waits for them, and re-layouts: none -> 13 us  [the longest x4 8.74 us: shards(): lax.dynamic_update_slice_in_dim(full, going_up, (here - far) % ways * ste...]
    ppermute x0 -> x7, starting transfers between devices: none -> 10.7 us  [the longest x3 7.05 us: shards(): lax.ppermute(going_down, 'ctx', [(d, (d - 1) % ways) for d in range(ways)])]
    while x34 -> x32, local copies, waits for them, and re-layouts: 16.9 us -> 7.89 us
  transfers between devices with their start and end apart: 6 -> 12, of which waited for: 3 -> 5; matrix products, arithmetic and copies ran while one was open for 8% -> 12% of each run, Pallas kernels for 0% -> 0%
where the time goes in v1:
time: 413 us; the launch traced here: 412 us
  waiting for transfers between devices  225 us (54%)
  matrix products  69.3 us (17%)
  local copies, waits for them, and re-layouts  50.5 us (12%)
  other arithmetic  18.8 us (5%)
  blocking collectives  18.6 us (5%)
  starting transfers between devices  15.1 us (4%)
  between operations  14.4 us (3%)
    reduce_scatter x1, waiting for transfers between devices, shards(): lax.psum_scatter(jnp.concatenate([grad_query, grad_keyval], axis=1), 'dp'...  154 us
    ppermute x4, waiting for transfers between devices, shards(): lax.ppermute(going_up, 'ctx', [(d, (d + 1) % ways) for d in range(ways)])  51.8 us
    all_gather x1, waiting for transfers between devices, shards(): lax.all_gather(jnp.concatenate([query_weight, keyval_matrix], axis=1), 'd...  19.4 us
    all_to_all x1, blocking collectives, shards(): lax.all_to_all(out_heads, 'ctx', split_axis=0, concat_axis=1, tiled=True)  18.6 us
    dot_general x2, matrix products, attend_part(): jnp.einsum('nhqkc,nkcd->nqhd', probs_b, vals, preferred_element_type=jnp....  13.1 us
    dot_general x1, matrix products, shards(): lax.dot_general(all_rows, dquery, contract, preferred_element_type=jnp.fl...  10.3 us
    dot_general x1, matrix products, shards(): jnp.dot(all_rows, jnp.concatenate([query_full, keyval_cols], axis=1), pre...  9.03 us
    dynamic_update_slice x4, local copies, waits for them, and re-layouts, shards(): lax.dynamic_update_slice_in_dim(full, going_up, (here - far) % ways * ste...  8.74 us
  transfers between devices with their start and end apart: 12, of which 5 were waited for; matrix products, arithmetic and copies ran while one was open for 12% of the time, Pallas kernels for 0%

profile of v1, /device:TPU:0, one launch (start us, length us, event | category | flops | bytes accessed | tf_op | source)
XLA Modules:
  0.0 412.5 jit_solution(5609485332407212902)
XLA Ops:
  7.2 2.6 pad_maximum_fusion.1
  10.3 2.9 collective-permute-start.1
  13.3 2.3 copy.101
  15.6 3.6 all-to-all-start
  21.4 13.2 %collective-permute-done = bf16[128,4096]{1,0:T(8,128)(2,1)} collective-permute-done((bf16[128,4096]{1,0:T(8,128)(2,1)}, bf16[128,4096]{1,0:T(8,128)(2,1)}, u32[]{:S(2)}, u32[]{:S(2)}) %collective-permute-start) | collective-permute-done | bytes 1048608 | tf_op jit(solution)/shard_map/ppermute | solution.py:101
  35.2 4.4 %broadcast_in_dim.43 = bf16[1024,4096]{1,0:T(8,128)(2,1)} broadcast(bf16[]{:T(256)} %constant.106.clone.1), dimensions={} | broadcast | bytes 8388610 | tf_op jit(solution)/shard_map/broadcast_in_dim | solution.py:97
  40.7 2.1 collective-permute-start.3
  42.7 25.4 %collective-permute-done.2 = bf16[128,4096]{1,0:T(8,128)(2,1)S(1)} collective-permute-done((bf16[128,4096]{1,0:T(8,128)(2,1)}, bf16[128,4096]{1,0:T(8,128)(2,1)S(1)}, u32[]{:S(2)}, u32[]{:S(2)}) %collective-permute-start.2) | collective-permute-done | bytes 1048608 | tf_op jit(solution)/shard_map/ppermute | solution.py:101
  68.9 2.3 constant_dynamic-update-slice_fusion.7
  72.3 2.0 collective-permute-start.5
  75.4 13.2 %collective-permute-done.4 = bf16[128,4096]{1,0:T(8,128)(2,1)} collective-permute-done((bf16[128,4096]{1,0:T(8,128)(2,1)S(1)}, bf16[128,4096]{1,0:T(8,128)(2,1)}, u32[]{:S(2)}, u32[]{:S(2)}) %collective-permute-start.4) | collective-permute-done | bytes 1048608 | tf_op jit(solution)/shard_map/ppermute | solution.py:101
  88.6 1.8 collective-permute-start.6
  91.5 19.4 %all-gather.2.cloned.1.call-done = bf16[4096,640]{1,0:T(8,128)(2,1)} async-done(((bf16[1024,640]{1,0:T(8,128)(2,1)}), bf16[4096,640]{1,0:T(8,128)(2,1)}) %all-gather.2.cloned.1.call-update) | async-done | bytes 5242896 | tf_op jit(solution)/shard_map/all_gather | solution.py:89
  111.0 1.3 slice.36
  112.3 2.4 constant_dynamic-update-slice_fusion.3
  115.8 2.9 constant_dynamic-update-slice_fusion.1
  119.5 9.0 %fusion.38 = bf16[1024,768]{1,0:T(8,128)(2,1)S(1)} fusion(bf16[1024,4096]{1,0:T(8,128)(2,1)} %constant_dynamic-update-slice_fusion.1, bf16[4096,256]{1,0:T(8,128)(2,1)S(1)} %maximum_select_fusion, bf16[4096,512]{1,0:T(8,128)(2,1)S(1)} %slice-done), kind=kOutput, calls=%fused_computation.49 | convolution fusion | flops 6455820288 | bytes 16252928 | tf_op jit(solution)/shard_map/dot_general | solution.py:118
  132.0 55.8 %while.16 = (s32[]{:T(128)}, bf16[2,4,128,4,128]{2,4,3,1,0:T(8,128)(2,1)}, bf16[2,4,128,4,128]{4,3,2,1,0:T(4,128)(2,1)}, f32[2,4,8,128,128]{4,3,2,1,0:T(8,128)},...) while((s32[]{:T(128)}, ...), condition=%wide.region_4.5_spmd, body=%wide.region_0.4_spmd.sunk | while | flops 3275222016 | bytes 217678256 | solution.py:62
  133.1 1.2 constant_dynamic-slice_fusion.5
  134.3 1.3 bitcast_reduce_fusion.2
  135.6 1.8 fusion.102
  137.4 2.3 bitcast_dynamic-update-slice_fusion.8
  139.7 1.9 copy-done.9
  142.4 6.5 %bitcast_dynamic-update-slice_fusion.6 = (bf16[2,4,128,4,128]{2,4,3,1,0:T(8,128)(2,1)}, bf16[4,128,4,128]{3,1,2,0:T(8,128)(2,1)S(1)}) fusion(bf16[2,4,128,4,128]{2,4,3,1,0:T(8,128)(2,1)} %get-tuple-element.241, s32[]{:T(128)} %get-tuple-element.240, bf16[4,8,128,128,1]{3,2,4,1,0:T(8,128)(2,1)S(1)} %bitcast.212, f32[4,4,128]{2,1,0:T(4,128)S(1)} %fusion.102, ...), kind=kOutput, calls=%fused_computation.27.clone.1 | convolution fusion | flops 547618816 | bytes 10502688 | tf_op jit(solution)/shard_map/while/body/eval_jaxpr/nhqkc,nkcd->nqhd/dot_general | solution.py:27
  149.0 1.2 multiply_reduce_fusion.2
  150.2 4.3 %fusion.103 = bf16[4,4,128,8,128]{2,4,1,3,0:T(8,128)(2,1)S(1)} fusion(f32[4,4,128]{2,1,0:T(4,128)S(1)} %bitcast.225, bf16[4,8,128,128,1]{3,2,4,1,0:T(8,128)(2,1)S(1)} %bitcast.213, bf16[2,4,128,4,128]{2,4,3,1,0:T(8,128)(2,1)} %copy-done.4, s32[]{:T(128)} %get-tuple-element.240, f32[4,4,128]{2,1,0:T(4,128)S(1)} %fusion.102, ...), kind=kOutput, calls=%fused_computation.5.clone.1 | convolution fusion | flops 553648128 | bytes 14180896 | tf_op jit(solution)/shard_map/while/body/eval_jaxpr/nqhd,nkcd->nhqkc/dot_general | solution.py:33
  154.6 1.3 bitcast_dynamic-update-slice_fusion.7
  155.9 2.0 copy-done.7
  160.8 1.2 constant_dynamic-slice_fusion.5
  162.1 1.3 bitcast_reduce_fusion.2
  163.4 1.8 fusion.102
  165.2 2.2 bitcast_dynamic-update-slice_fusion.8
  167.5 1.9 copy-done.9
  170.2 6.5 %bitcast_dynamic-update-slice_fusion.6 = (bf16[2,4,128,4,128]{2,4,3,1,0:T(8,128)(2,1)}, bf16[4,128,4,128]{3,1,2,0:T(8,128)(2,1)S(1)}) fusion(bf16[2,4,128,4,128]{2,4,3,1,0:T(8,128)(2,1)} %get-tuple-element.241, s32[]{:T(128)} %get-tuple-element.240, bf16[4,8,128,128,1]{3,2,4,1,0:T(8,128)(2,1)S(1)} %bitcast.212, f32[4,4,128]{2,1,0:T(4,128)S(1)} %fusion.102, ...), kind=kOutput, calls=%fused_computation.27.clone.1 | convolution fusion | flops 547618816 | bytes 10502688 | tf_op jit(solution)/shard_map/while/body/eval_jaxpr/nhqkc,nkcd->nqhd/dot_general | solution.py:27
  176.8 1.2 multiply_reduce_fusion.2
  178.0 4.3 %fusion.103 = bf16[4,4,128,8,128]{2,4,1,3,0:T(8,128)(2,1)S(1)} fusion(f32[4,4,128]{2,1,0:T(4,128)S(1)} %bitcast.225, bf16[4,8,128,128,1]{3,2,4,1,0:T(8,128)(2,1)S(1)} %bitcast.213, bf16[2,4,128,4,128]{2,4,3,1,0:T(8,128)(2,1)} %copy-done.4, s32[]{:T(128)} %get-tuple-element.240, f32[4,4,128]{2,1,0:T(4,128)S(1)} %fusion.102, ...), kind=kOutput, calls=%fused_computation.5.clone.1 | convolution fusion | flops 553648128 | bytes 14180896 | tf_op jit(solution)/shard_map/while/body/eval_jaxpr/nqhd,nkcd->nhqkc/dot_general | solution.py:33
  182.4 1.3 bitcast_dynamic-update-slice_fusion.7
  183.7 2.0 copy-done.7
  187.8 7.2 %fusion.41 = f32[8,128,128]{2,0,1:T(8,128)S(1)} fusion(f32[8,8,128,128]{3,2,1,0:T(8,128)} %bitcast.219, s32[8,8]{0,1:T(8,128)S(1)} %copy-done.14, pred[8,8]{0,1:T(8,128)(4,1)S(1)} %copy-done.15), kind=kOutput, calls=%fused_computation.54 | convolution fusion | flops 100664320 | bytes 4718912 | tf_op jit(solution)/shard_map/bnk,nkcd->bcd/dot_general | solution.py:71
  195.2 5.0 %fusion.44 = f32[8,128,128]{2,0,1:T(8,128)S(1)} fusion(f32[8,8,128,128]{3,2,1,0:T(8,128)S(1)} %bitcast.220, s32[8,8]{0,1:T(8,128)S(1)} %copy-done.14, pred[8,8]{0,1:T(8,128)(4,1)S(1)} %copy-done.15), kind=kOutput, calls=%fused_computation.55 | convolution fusion | flops 100664320 | bytes 4718912 | tf_op jit(solution)/shard_map/bnk,nkcd->bcd/dot_general | solution.py:72
  201.0 10.3 %fusion.47 = f32[4096,512]{0,1:T(8,128)} fusion(bf16[1024,4096]{1,0:T(8,128)(2,1)} %constant_dynamic-update-slice_fusion.1, bf16[128,8,4,128]{3,2,1,0:T(4,128)(2,1)S(1)} %bitcast.227), kind=kOutput, calls=%fused_computation.56 | convolution fusion | flops 4294967296 | bytes 17825792 | tf_op jit(solution)/shard_map/dot_general | solution.py:138
  211.3 4.7 %fusion.53 = f32[4096,128]{0,1:T(8,128)S(1)} fusion(bf16[1024,4096]{1,0:T(8,128)(2,1)} %constant_dynamic-update-slice_fusion.1, s32[]{:T(128)S(6)} %select_n.118, f32[1024,128]{1,0:T(8,128)S(1)} %bitcast.216, f32[1024,128]{1,0:T(8,128)S(1)} %bitcast.218, f32[1024,256]{1,0:T(8,128)S(1)} %collective-permute-done.8), kind=kOutput, calls=%fused_computation.62 | convolution fusion | flops 1074135040 | bytes 12058628 | tf_op jit(solution)/shard_map/dot_general | solution.py:139
  216.0 8.6 %pad_maximum_fusion = f32[4096,640]{0,1:T(8,128)} fusion(f32[4096,128]{0,1:T(8,128)S(1)} %fusion.53, f32[4096,512]{0,1:T(8,128)} %fusion.47), kind=kLoop, calls=%fused_computation.39 | loop fusion | flops 2621440 | bytes 20971520 | tf_op jit(solution)/shard_map/concatenate | solution.py:141
  226.4 18.6 %all_to_all.32 = bf16[8,128,512]{2,1,0:T(8,128)(2,1)S(1)} all-to-all(bf16[8,128,512]{2,1,0:T(8,128)(2,1)S(1)} %copy.102), channel_id=1, replica_groups=mesh['ctx'=8,'dp'=4] {'ctx'}, dimensions={0} | all-to-all | bytes 2097152 | tf_op jit(solution)/shard_map/all_to_all | solution.py:130
  245.7 1.3 copy.73
  247.0 154.0 %reduce-scatter.2.cloned.1.call-done = f32[1024,640]{0,1:T(8,128)} async-done(((f32[4096,640]{0,1:T(8,128)}), f32[1024,640]{0,1:T(8,128)}) %reduce-scatter.2.cloned.1.call-update) | async-done | bytes 2621456 | tf_op jit(solution)/shard_map/reduce_scatter | solution.py:140
  401.0 1.8 slice.40
  402.8 1.8 copy.74
  (110 shorter events, 25.5 us)
Async XLA Ops:
  7.2 13.6 %copy-start = (s32[4,8,8]{2,1,0:T(8,128)S(1)}, s32[4,8,8]{2,1,0:T(8,128)}, u32[]{:S(2)}) copy-start(s32[4,8,8]{2,1,0:T(8,128)} %param.12) | copy-start | bytes 3076
  7.2 32.4 %copy-start.12 = (bf16[1,128,4096]{2,1,0:T(8,128)(2,1)S(1)}, bf16[1,128,4096]{2,1,0:T(8,128)(2,1)}, u32[]{:S(2)}) copy-start(bf16[1,128,4096]{2,1,0:T(8,128)(2,1)} %param.8) | copy-start | bytes 3145732
  7.2 103.8 %all-gather.2.cloned.1.call-start = ((), (), s32[]{:S(2)}) async-start(), calls=%async_computation.3 | async-start | bytes 6553600 | tf_op jit(solution)/shard_map/all_gather | solution.py:89
  9.8 24.8 %collective-permute-start = (bf16[128,4096]{1,0:T(8,128)(2,1)}, bf16[128,4096]{1,0:T(8,128)(2,1)}, u32[]{:S(2)}, u32[]{:S(2)}) collective-permute-start(bf16[128,4096]{1,0:T(8,128)(2,1)} %bitcast.222), channel_id=1, source_target_pairs={{0,4},{4,8},{8,12},{12,16},{16,20},{20,24},{24,28},{28,0},{1,5},{5... | collective-permute-start | bytes 3145736 | tf_op jit(solution)/shard_map/ppermute | solution.py:101
  10.3 30.4 %collective-permute-start.1 = (bf16[128,4096]{1,0:T(8,128)(2,1)}, bf16[128,4096]{1,0:T(8,128)(2,1)S(1)}, u32[]{:S(2)}, u32[]{:S(2)}) collective-permute-start(bf16[128,4096]{1,0:T(8,128)(2,1)} %bitcast.223), channel_id=1, source_target_pairs={{0,28},{4,0},{8,4},{12,8},{16,12},{20,16},{24,20},{28,24},{1,29},{... | collective-permute-start | bytes 3145736 | tf_op jit(solution)/shard_map/ppermute | solution.py:104
  15.6 116.4 %all-to-all-start = ((bf16[128,8,512]{0,2,1:T(8,128)(2,1)}), bf16[128,8,512]{0,2,1:T(8,128)(2,1)S(1)}, u32[]{:S(2)}, u32[]{:S(2)}) async-start(bf16[128,8,512]{0,2,1:T(8,128)(2,1)} %bitcast.38), calls=%async_computation | async-start | bytes 2097152 | tf_op jit(solution)/shard_map/all_to_all | solution.py:125
  19.1 381.9 %reduce-scatter.2.cloned.1.call-start = ((), (), s32[]{:S(2)}) async-start(), calls=%async_computation.4 | async-start | bytes 13107200 | tf_op jit(solution)/shard_map/reduce_scatter | solution.py:140
  34.6 33.6 %collective-permute-start.2 = (bf16[128,4096]{1,0:T(8,128)(2,1)}, bf16[128,4096]{1,0:T(8,128)(2,1)S(1)}, u32[]{:S(2)}, u32[]{:S(2)}) collective-permute-start(bf16[128,4096]{1,0:T(8,128)(2,1)} %collective-permute-done), channel_id=1, source_target_pairs={{0,4},{4,8},{8,12},{12,16},{16,20},{20,24},{24,28},{28,0},{1,5},{5... | collective-permute-start | bytes 3145736 | tf_op jit(solution)/shard_map/ppermute | solution.py:101
  40.7 31.6 %collective-permute-start.3 = (bf16[128,4096]{1,0:T(8,128)(2,1)S(1)}, bf16[128,4096]{1,0:T(8,128)(2,1)S(1)}, u32[]{:S(2)}, u32[]{:S(2)}) collective-permute-start(bf16[128,4096]{1,0:T(8,128)(2,1)S(1)} %collective-permute-done.1), channel_id=1, source_target_pairs={{0,28},{4,0},{8,4},{12,8},{16,12},{20,16},{24,20},{28,24},{1,29},{... | collective-permute-start | bytes 3145736 | tf_op jit(solution)/shard_map/ppermute | solution.py:104
  68.2 20.4 %collective-permute-start.4 = (bf16[128,4096]{1,0:T(8,128)(2,1)S(1)}, bf16[128,4096]{1,0:T(8,128)(2,1)}, u32[]{:S(2)}, u32[]{:S(2)}) collective-permute-start(bf16[128,4096]{1,0:T(8,128)(2,1)S(1)} %collective-permute-done.2), channel_id=1, source_target_pairs={{0,4},{4,8},{8,12},{12,16},{16,20},{20,24},{24,28},{28,0},{1,5},{5... | collective-permute-start | bytes 3145736 | tf_op jit(solution)/shard_map/ppermute | solution.py:101
  72.3 42.5 %collective-permute-start.5 = (bf16[128,4096]{1,0:T(8,128)(2,1)S(1)}, bf16[128,4096]{1,0:T(8,128)(2,1)S(1)}, u32[]{:S(2)}, u32[]{:S(2)}) collective-permute-start(bf16[128,4096]{1,0:T(8,128)(2,1)S(1)} %collective-permute-done.3), channel_id=1, source_target_pairs={{0,28},{4,0},{8,4},{12,8},{16,12},{20,16},{24,20},{28,24},{1,29},{... | collective-permute-start | bytes 3145736 | tf_op jit(solution)/shard_map/ppermute | solution.py:104
  88.6 27.2 %collective-permute-start.6 = (bf16[128,4096]{1,0:T(8,128)(2,1)}, bf16[128,4096]{1,0:T(8,128)(2,1)}, u32[]{:S(2)}, u32[]{:S(2)}) collective-permute-start(bf16[128,4096]{1,0:T(8,128)(2,1)} %collective-permute-done.4), channel_id=1, source_target_pairs={{0,4},{4,8},{8,12},{12,16},{16,20},{20,24},{24,28},{28,0},{1,5},{5... | collective-permute-start | bytes 3145736 | tf_op jit(solution)/shard_map/ppermute | solution.py:101
  112.3 6.4 %collective-permute-start.7 = (bf16[4096,128]{1,0:T(8,128)(2,1)S(1)}, bf16[4096,128]{1,0:T(8,128)(2,1)S(1)}, u32[]{:S(2)}, u32[]{:S(2)}) collective-permute-start(bf16[4096,128]{1,0:T(8,128)(2,1)S(1)} %slice.36), channel_id=1, source_target_pairs={{0,4},{4,0},{8,12},{12,8},{16,20},{20,16},{24,28},{28,24},{1,5},{5... | collective-permute-start | bytes 3145736 | tf_op jit(solution)/shard_map/ppermute | solution.py:14
  114.8 4.7 %slice-start = ((bf16[4096,640]{1,0:T(8,128)(2,1)}), bf16[4096,512]{1,0:T(8,128)(2,1)S(1)}, s32[]{:S(2)}) async-start(bf16[4096,640]{1,0:T(8,128)(2,1)} %all-gather.2.cloned.1.call-done), calls=%async_computation.5 | async-start | bytes 8388608 | tf_op jit(solution)/shard_map/slice | solution.py:92
  128.5 1.1 copy-start.11
  131.9 55.8 %copy-start.14 = (s32[8,8]{0,1:T(8,128)S(1)}, s32[8,8]{0,1:T(8,128)}, u32[]{:S(2)}) copy-start(s32[8,8]{0,1:T(8,128)} %copy.68) | copy-start | bytes 772
  132.0 55.8 %copy-start.15 = (pred[8,8]{0,1:T(8,128)(4,1)S(1)}, pred[8,8]{0,1:T(8,128)(4,1)}, u32[]{:S(2)}) copy-start(pred[8,8]{0,1:T(8,128)(4,1)} %iota_compare_fusion.1) | copy-start | bytes 196
  132.2 5.3 %copy-start.4 = (bf16[2,4,128,4,128]{2,4,3,1,0:T(8,128)(2,1)}, bf16[2,4,128,4,128]{2,4,3,1,0:T(8,128)(2,1)S(1)}, u32[]{:S(2)}) copy-start(bf16[2,4,128,4,128]{2,4,3,1,0:T(8,128)(2,1)S(1)} %get-tuple-element.262) | copy-start | bytes 3145732 | tf_op jit(solution)/shard_map/while
  134.3 3.1 copy-start.8
  135.6 4.1 %copy-start.2 = (f32[4,8,128,128,4]{3,2,4,1,0:T(8,128)}, f32[4,8,128,128,4]{3,2,4,1,0:T(8,128)S(1)}, u32[]{:S(2)}) copy-start(f32[4,8,128,128,4]{3,2,4,1,0:T(8,128)S(1)} %get-tuple-element.224) | copy-start | bytes 25165828 | tf_op jit(solution)/shard_map/while
  139.7 1.9 copy-start.9
  142.4 7.8 %copy-start.3 = (f32[4,8,128,128,4]{3,2,4,1,0:T(8,128)S(1)}, f32[4,8,128,128,4]{3,2,4,1,0:T(8,128)}, u32[]{:S(2)}) copy-start(f32[4,8,128,128,4]{3,2,4,1,0:T(8,128)} %copy-done.2) | copy-start | bytes 25165828 | tf_op jit(solution)/shard_map/while
  150.2 4.4 %copy-start.6 = (f32[2,4,8,128,128]{4,3,2,1,0:T(8,128)S(1)}, f32[2,4,8,128,128]{4,3,2,1,0:T(8,128)}, u32[]{:S(2)}) copy-start(f32[2,4,8,128,128]{4,3,2,1,0:T(8,128)} %get-tuple-element.243) | copy-start | bytes 12582916 | tf_op jit(solution)/shard_map/while
  154.6 5.4 %copy-start.5 = (bf16[2,4,128,4,128]{2,4,3,1,0:T(8,128)(2,1)S(1)}, bf16[2,4,128,4,128]{2,4,3,1,0:T(8,128)(2,1)}, u32[]{:S(2)}) copy-start(bf16[2,4,128,4,128]{2,4,3,1,0:T(8,128)(2,1)} %copy-done.4) | copy-start | bytes 3145732 | tf_op jit(solution)/shard_map/while
  155.9 2.0 copy-start.7
  160.0 5.2 %copy-start.4 = (bf16[2,4,128,4,128]{2,4,3,1,0:T(8,128)(2,1)}, bf16[2,4,128,4,128]{2,4,3,1,0:T(8,128)(2,1)S(1)}, u32[]{:S(2)}) copy-start(bf16[2,4,128,4,128]{2,4,3,1,0:T(8,128)(2,1)S(1)} %get-tuple-element.262) | copy-start | bytes 3145732 | tf_op jit(solution)/shard_map/while
  162.1 3.2 copy-start.8
  163.4 4.1 %copy-start.2 = (f32[4,8,128,128,4]{3,2,4,1,0:T(8,128)}, f32[4,8,128,128,4]{3,2,4,1,0:T(8,128)S(1)}, u32[]{:S(2)}) copy-start(f32[4,8,128,128,4]{3,2,4,1,0:T(8,128)S(1)} %get-tuple-element.224) | copy-start | bytes 25165828 | tf_op jit(solution)/shard_map/while
  167.5 1.9 copy-start.9
  170.2 7.8 %copy-start.3 = (f32[4,8,128,128,4]{3,2,4,1,0:T(8,128)S(1)}, f32[4,8,128,128,4]{3,2,4,1,0:T(8,128)}, u32[]{:S(2)}) copy-start(f32[4,8,128,128,4]{3,2,4,1,0:T(8,128)} %copy-done.2) | copy-start | bytes 25165828 | tf_op jit(solution)/shard_map/while
  178.0 4.4 %copy-start.6 = (f32[2,4,8,128,128]{4,3,2,1,0:T(8,128)S(1)}, f32[2,4,8,128,128]{4,3,2,1,0:T(8,128)}, u32[]{:S(2)}) copy-start(f32[2,4,8,128,128]{4,3,2,1,0:T(8,128)} %get-tuple-element.243) | copy-start | bytes 12582916 | tf_op jit(solution)/shard_map/while
  182.3 5.4 %copy-start.5 = (bf16[2,4,128,4,128]{2,4,3,1,0:T(8,128)(2,1)S(1)}, bf16[2,4,128,4,128]{2,4,3,1,0:T(8,128)(2,1)}, u32[]{:S(2)}) copy-start(bf16[2,4,128,4,128]{2,4,3,1,0:T(8,128)(2,1)} %copy-done.4) | copy-start | bytes 3145732 | tf_op jit(solution)/shard_map/while
  183.6 2.0 copy-start.7
  187.8 7.4 %copy-start.10 = (f32[2,4,8,128,128]{4,3,2,1,0:T(8,128)S(1)}, f32[2,4,8,128,128]{4,3,2,1,0:T(8,128)}, u32[]{:S(2)}) copy-start(f32[2,4,8,128,128]{4,3,2,1,0:T(8,128)} %get-tuple-element.66) | copy-start | bytes 12582916
  187.8 13.2 %copy-start.16 = (bf16[2,4,128,4,128]{4,3,2,1,0:T(4,128)(2,1)S(1)}, bf16[2,4,128,4,128]{4,3,2,1,0:T(4,128)(2,1)}, u32[]{:S(2)}) copy-start(bf16[2,4,128,4,128]{4,3,2,1,0:T(4,128)(2,1)} %get-tuple-element.64) | copy-start | bytes 3145732
  200.3 10.9 %collective-permute-start.8 = (f32[1024,256]{1,0:T(8,128)S(1)}, f32[1024,256]{1,0:T(8,128)S(1)}, u32[]{:S(2)}, u32[]{:S(2)}) collective-permute-start(f32[1024,256]{1,0:T(8,128)S(1)} %pad_maximum_fusion.2), channel_id=1, source_target_pairs={{0,4},{4,0},{8,12},{12,8},{16,20},{20,16},{24,28},{28,24},{1,5},{5... | collective-permute-start | bytes 3145736 | tf_op jit(solution)/shard_map/ppermute | solution.py:14
  224.7 1.2 copy-start.13
  225.9 179.7 %copy-start.1 = (s32[4,8,8]{2,1,0:T(8,128)S(1)}, s32[4,8,8]{2,1,0:T(8,128)}, u32[]{:S(2)}) copy-start(s32[4,8,8]{2,1,0:T(8,128)} %param.12) | copy-start | bytes 3076
  401.0 3.6 slice-start.1
Sparse Core Ops, SparseCore 0:
  10.2 100.7 all-gather.1
  224.8 176.1 reduce-scatter.1
